TPU v7x, 256 devices: a whole 4x4x8 slice. The times are simulated.
256 devices in a mesh: rows: 32 (over y, x, core), cols: 8 (over z).
Axes of the slice: x: 4, y: 4, z: 8, core: 2. Of those that a mesh axis runs over, the one named last changes fastest.
Arguments:
- sheet: bfloat16 [16, 4096, 1024], P('cols', 'rows'), may hold values from -600 to 600
- w_in: bfloat16 [1024, 16, 384], P(None, 'cols'), may hold values from -0.1875 to 0.1875
- w_out: bfloat16 [16, 128, 1024], P('cols'), may hold values from -0.125 to 0.125
Outputs:
- mixed: bfloat16 [16, 4096, 1024], P('cols', 'rows')
All inputs are finite; a program needn't handle non-finite values.
Results may differ from a plain program's by a relative error of at most 0.0067.
Values may be sent and summed in bfloat16 or wider, within the bound.
No kernel may reach another device: no remote copies, remote signals or barrier semaphores. Data moves between devices by JAX's collectives and lax.ppermute only.
A program may use at most 128 MiB of HBM per device.

v0:
```python
import jax
import jax.numpy as jnp
import numpy as np
from jax import lax
from jax.sharding import Mesh, PartitionSpec as P

ROWS_AXES = ("y", "x", "core")


def head_norm(values):
    return values * lax.rsqrt(jnp.mean(values * values, axis=-1, keepdims=True) + 1e-06)


def feature_map(values):
    return jax.nn.elu(values) + 1.0


def finish_proj(proj):
    parts = [
        head_norm(proj[..., 0, :]),
        head_norm(proj[..., 1, :]),
        proj[..., 2, :],
        feature_map(proj[..., 3, :]),
        feature_map(proj[..., 4, :]),
        proj[..., 5, :],
    ]
    return jnp.stack(parts, axis=-2).astype(jnp.bfloat16)


def masked_prefix(gathered, mine):
    idx = lax.broadcasted_iota(jnp.int32, gathered.shape, 0)
    before = jnp.sum(jnp.where(idx < mine, gathered, 0.0), axis=0)
    return (before, jnp.sum(gathered, axis=0))


def exclusive_rows_scan(states):
    core = lax.axis_index("core")
    pair = lax.all_gather(states, "core")
    total = pair[0] + pair[1]
    own = jnp.where(core == 1, pair[0], jnp.zeros_like(pair[0]))
    half = total.shape[0] // 2
    mine = lax.dynamic_slice_in_dim(total, core * half, half, axis=0)
    gx = lax.all_gather(mine, "x")
    xpre, xsum = masked_prefix(gx, lax.axis_index("x"))
    gy = lax.all_gather(xsum, "y")
    ypre, _ = masked_prefix(gy, lax.axis_index("y"))
    chip_prefix = lax.all_gather(ypre + xpre, "core", axis=0, tiled=True)
    return chip_prefix + own


def body(sheet, w_in, w_out):
    high = lax.Precision.HIGHEST
    width = sheet.shape[2]
    heads_here = w_in.shape[1]
    hdim = w_out.shape[1] // 2
    ncols = lax.axis_size("cols")
    core = lax.axis_index("core")
    wh = width // 2
    w_part = lax.dynamic_slice_in_dim(w_out, core * wh, wh, axis=2)
    w_part = lax.all_gather(w_part, "cols", axis=0, tiled=True)
    w_full = lax.all_gather(w_part, "core", axis=2, tiled=True)
    xloc = sheet.astype(jnp.float32)
    normed = (xloc * lax.rsqrt(jnp.mean(xloc * xloc, axis=-1, keepdims=True) + 1e-06)).astype(
        jnp.bfloat16
    )
    piece = lax.all_gather(normed, "cols", axis=0, tiled=True)
    w_flat = w_in.reshape(width, heads_here * 6 * hdim)
    proj = jnp.dot(piece.reshape(-1, width), w_flat, preferred_element_type=jnp.float32)
    all_cols, row_count = (piece.shape[0], piece.shape[1])
    parts = finish_proj(proj.reshape(all_cols, row_count, heads_here, 6, hdim))
    qrow, krow, vrow = (parts[:, :, :, 0], parts[:, :, :, 1], parts[:, :, :, 2])
    fq, fk, vcol = (parts[:, :, :, 3], parts[:, :, :, 4], parts[:, :, :, 5])
    states = jnp.einsum("crhk,crhv->chkv", fk, vcol, preferred_element_type=jnp.float32)
    prior = exclusive_rows_scan(states)
    scale = hdim ** (-0.5)
    score = jnp.einsum("crhd,erhd->rhce", qrow, krow, preferred_element_type=jnp.float32) * scale
    expo = jnp.exp(score)
    weights = (expo / jnp.sum(expo, axis=-1, keepdims=True)).astype(jnp.bfloat16)
    orow = jnp.einsum("rhce,erhd->crhd", weights, vrow, preferred_element_type=jnp.float32).astype(
        jnp.bfloat16
    )
    causal = (jnp.arange(row_count)[:, None] >= jnp.arange(row_count)[None, :]).astype(jnp.float32)
    inner = jnp.einsum("cthd,cshd->chts", fq, fk, preferred_element_type=jnp.float32) * causal
    local = jnp.einsum("chts,cshv->cthv", inner, vcol.astype(jnp.float32), precision=high)
    carried = jnp.einsum("cthk,chkv->cthv", fq.astype(jnp.float32), prior, precision=high)
    ocol = head_norm(carried + local).astype(jnp.bfloat16)
    results = jnp.concatenate([orow, ocol], axis=3)
    mine = lax.all_to_all(results, "cols", 0, 2, tiled=True)
    own_cols = mine.shape[0]
    mixed = jnp.dot(
        mine.reshape(own_cols * row_count, -1),
        w_full.reshape(-1, width),
        preferred_element_type=jnp.float32,
    )
    return mixed.reshape(own_cols, row_count, width).astype(jnp.bfloat16)


def split_mesh(mesh):
    devs = mesh.devices
    n_rows, n_cols = devs.shape
    try:
        nx = len({d.coords[0] for d in devs.flat})
    except Exception:
        nx = 4
    ny = n_rows // (nx * 2)
    return Mesh(devs.reshape(ny, nx, 2, n_cols), ROWS_AXES + ("cols",))


def solution(mesh):
    m4 = split_mesh(mesh)
    spec = P("cols", ROWS_AXES, None)
    return jax.shard_map(
        body,
        mesh=m4,
        in_specs=(spec, P(None, "cols", None), P("cols", None, None)),
        out_specs=spec,
        check_vma=False,
    )
```

profile of v0, /device:TPU:2, one launch (start us, length us, event | category | flops | bytes accessed | tf_op | source)
XLA Modules:
  0.0 267.3 jit_solution(8593396329968372122)
XLA Ops:
  6.5 0.0 copy-start
  6.5 0.0 all-gather.10.cloned.1.call-start
  6.5 1.3 fusion.10
  7.8 2.0 fusion.11
  9.8 0.0 all-gather.10.cloned.1.call-update
  9.8 0.0 all-gather.16.cloned.1.call-start
  9.9 1.7 copy.59
  11.6 1.6 copy.38
  13.3 54.4 %all-gather.10.cloned.1.call-done = bf16[16,128,1024]{2,1,0:T(8,128)(2,1)} async-done(((bf16[2,128,1024]{2,1,0:T(8,128)(2,1)}), bf16[16,128,1024]{2,1,0:T(8,128)(2,1)}) %all-gather.10.cloned.1.call-update) | async-done | bytes 4194320 | tf_op jit(solution)/shard_map/all_gather | solution.py:66
  67.7 5.8 %fusion.43 = (bf16[16,128,2,6,64]{1,4,3,2,0:T(8,128)(2,1)S(1)}, f32[16,128,2,6,64]{1,4,3,2,0:T(8,128)S(1)}) fusion(bf16[2,6,64,1024,1]{3,2,1,0,4:T(8,128)(2,1)} %bitcast.62, bf16[16,128,1024]{2,1,0:T(8,128)(2,1)} %all-gather.10.cloned.1.call-done), kind=kOutput, calls=%fused_computation.67 | convolution fusion | flops 3222798336 | bytes 15204352 | tf_op jit(solution)/shard_map/dot_general | solution.py:68
  73.5 0.0 copy-start.2
  73.5 0.0 copy-start.5
  73.5 2.6 copy-done.2
  76.2 1.0 copy-done.5
  77.1 1.5 fusion.26
  78.7 0.0 all-gather.16.cloned.1.call-update
  78.7 0.0 all-gather.20.cloned.1.call-start
  78.7 14.6 %all-gather.16.cloned.1.call-done = f32[32,2,64,64]{3,2,1,0:T(8,128)} async-done(((f32[16,2,64,64]{3,2,1,0:T(8,128)}), f32[32,2,64,64]{3,2,1,0:T(8,128)}) %all-gather.16.cloned.1.call-update) | async-done | bytes 1048592 | tf_op jit(solution)/shard_map/all_gather | solution.py:38
  93.4 1.7 fusion.42
  95.0 0.9 dynamic-slice_add_fusion
  95.9 0.0 all-gather.20.cloned.1.call-update
  95.9 0.0 all-gather.12.cloned.1.call-start
  96.0 0.0 copy-done
  96.0 0.8 constant_dynamic-slice_fusion
  96.7 0.0 all-gather.12.cloned.1.call-update
  96.8 0.0 all-gather.18.cloned.1.call-start
  96.8 32.9 %all-gather.20.cloned.1.call-done = f32[32,2,64,64]{3,2,1,0:T(8,128)} async-done(((f32[8,2,64,64]{3,2,1,0:T(8,128)}), f32[32,2,64,64]{3,2,1,0:T(8,128)}) %all-gather.20.cloned.1.call-update) | async-done | bytes 1048592 | tf_op jit(solution)/shard_map/all_gather | solution.py:43
  129.7 3.1 %select_reduce_fusion = (f32[8,2,64,64]{3,2,1,0:T(8,128)}, f32[8,2,64,64]{3,2,1,0:T(8,128)}) fusion(f32[4,8,2,64,64]{4,3,2,1,0:T(8,128)} %bitcast.59, pred[4]{0:T(512)(128)(4,1)S(1)} %iota_compare_fusion.1), kind=kLoop, calls=%fused_computation.8 | loop fusion | flops 655360 | bytes 1572868 | tf_op jit(solution)/shard_map/reduce_sum | solution.py:32
  132.8 0.0 all-gather.18.cloned.1.call-update
  132.8 0.2 all-gather.14.cloned.1.call-start
  133.1 40.2 %all-gather.12.cloned.1.call-done = bf16[16,128,512]{2,1,0:T(8,128)(2,1)} async-done(((bf16[2,128,512]{2,1,0:T(8,128)(2,1)}), bf16[16,128,512]{2,1,0:T(8,128)(2,1)}) %all-gather.12.cloned.1.call-update) | async-done | bytes 2097168 | tf_op jit(solution)/shard_map/all_gather | solution.py:60
  173.3 0.0 all-gather.14.cloned.1.call-update
  173.3 1.9 multiply_reduce_fusion.1
  175.2 1.1 slice_bitcast_fusion.1
  176.3 1.9 fusion.21
  178.2 2.5 copy.43
  180.7 2.5 copy.44
  183.2 2.2 fusion.44
  185.5 1.3 copy.45
  186.8 0.1 fusion.27
  186.9 0.1 divide_convert_fusion
  187.0 1.4 copy.47
  188.4 1.6 copy.46
  190.1 1.7 fusion.45
  191.7 3.0 %copy.48 = bf16[128,2,64,16]{0,2,1,3:T(8,128)(2,1)} copy(bf16[128,2,64,16]{2,3,1,0:T(8,128)(2,1)} %fusion.45) | data formatting | bytes 1048576 | tf_op jit(solution)/shard_map/rhce,erhd->crhd/dot_general | solution.py:79
  194.7 2.6 fusion.37
  197.4 0.0 copy-start.3
  197.4 9.5 %all-gather.18.cloned.1.call-done = f32[32,2,64,64]{3,2,1,0:T(8,128)} async-done(((f32[8,2,64,64]{3,2,1,0:T(8,128)}), f32[32,2,64,64]{3,2,1,0:T(8,128)}) %all-gather.18.cloned.1.call-update) | async-done | bytes 1048592 | tf_op jit(solution)/shard_map/all_gather | solution.py:45
  206.9 2.0 select_reduce_fusion.1
  208.8 0.0 copy-start.1
  208.8 0.0 copy-done.3
  208.8 0.1 add.72
  208.9 2.9 %all_gather.34 = f32[16,2,64,64]{3,2,1,0:T(8,128)S(1)} all-gather(f32[8,2,64,64]{3,2,1,0:T(8,128)S(1)} %add.72), channel_id=1, replica_groups=mesh['y'=4,'x'=4,'core'=2,'cols'=8] {'core'}, dimensions={0}, use_global_device_ids=true | all-gather | bytes 786432 | tf_op jit(solution)/shard_map/all_gather | solution.py:47
  211.8 0.0 copy-done.1
  211.8 2.6 fusion.18
  214.4 3.3 %multiply_reduce_fusion = (f32[16,128,2]{1,2,0:T(2,128)S(1)}, f32[16,128,2,64]{1,3,2,0:T(8,128)S(1)}) fusion(f32[16,2,64,128]{3,2,1,0:T(8,128)S(1)} %fusion.18, f32[16,2,128,128]{3,2,1,0:T(8,128)S(1)} %fusion.37, f32[128,128]{1,0:T(8,128)S(1)} %fusion.28, bf16[16,128,2,6,64]{1,4,3,2,0:T(8,128)(2,1)} %copy-done.5), kind=kOutput, calls=%fused_computation.28 | convolution fusion | flops 403959808 | bytes 4800512 | tf_op jit(solution)/shard_map/chts,cshv->cthv/dot_general | solution.py:84
  217.8 0.1 multiply_convert_fusion
  217.9 0.1 pad_maximum_fusion
  218.0 0.8 copy.53
  218.8 35.8 %all_to_all.15 = bf16[16,128,2,128]{3,2,1,0:T(2,128)(2,1)S(1)} all-to-all(bf16[16,128,2,128]{3,2,1,0:T(2,128)(2,1)S(1)} %copy.53), channel_id=1, replica_groups=mesh['y'=4,'x'=4,'core'=2,'cols'=8] {'cols'}, dimensions={0} | all-to-all | bytes 2097152 | tf_op jit(solution)/shard_map/all_to_all | solution.py:88
  254.7 0.7 copy.76
  255.4 0.8 dot_general.39
  256.2 0.0 all-gather.14.cloned.1.call-done
  256.3 4.2 %convolution_convert_fusion = bf16[2,128,1024]{2,1,0:T(8,128)(2,1)} fusion(bf16[2,128,2048]{2,1,0:T(8,128)(2,1)S(1)} %dot_general.39, bf16[2048,1024,1]{1,0,2:T(8,128)(2,1)} %bitcast.63), kind=kOutput, calls=%fused_computation.14 | convolution fusion | flops 1074003968 | bytes 5767168 | tf_op jit(solution)/shard_map/dot_general | solution.py:90
  (11 shorter events, 0.1 us)
Async XLA Ops:
  6.5 89.4 %copy-start = (bf16[2,128,1024]{2,1,0:T(8,128)(2,1)S(1)}, bf16[2,128,1024]{2,1,0:T(8,128)(2,1)}, u32[]{:S(2)}) copy-start(bf16[2,128,1024]{2,1,0:T(8,128)(2,1)} %param.5) | copy-start | bytes 1572868
  6.5 61.2 %all-gather.10.cloned.1.call-start = ((), (), s32[]{:S(2)}) async-start(), calls=%async_computation.1 | async-start | bytes 4718592 | tf_op jit(solution)/shard_map/all_gather | solution.py:66
  9.8 83.5 %all-gather.16.cloned.1.call-start = ((), (), s32[]{:S(2)}) async-start(), calls=%async_computation.4 | async-start | bytes 3145728 | tf_op jit(solution)/shard_map/all_gather | solution.py:38
  73.5 2.7 copy-start.2
  73.5 3.6 %copy-start.5 = (bf16[16,128,2,6,64]{1,4,3,2,0:T(8,128)(2,1)}, bf16[16,128,2,6,64]{1,4,3,2,0:T(8,128)(2,1)S(1)}, u32[]{:S(2)}) copy-start(bf16[16,128,2,6,64]{1,4,3,2,0:T(8,128)(2,1)S(1)} %get-tuple-element.13) | copy-start | bytes 9437188
  78.7 51.0 %all-gather.20.cloned.1.call-start = ((), (), s32[]{:S(2)}) async-start(), calls=%async_computation.6 | async-start | bytes 2621440 | tf_op jit(solution)/shard_map/all_gather | solution.py:43
  95.9 77.3 %all-gather.12.cloned.1.call-start = ((), (), s32[]{:S(2)}) async-start(), calls=%async_computation.2 | async-start | bytes 2359296 | tf_op jit(solution)/shard_map/all_gather | solution.py:60
  96.8 110.1 %all-gather.18.cloned.1.call-start = ((), (), s32[]{:S(2)}) async-start(), calls=%async_computation.5 | async-start | bytes 2621440 | tf_op jit(solution)/shard_map/all_gather | solution.py:45
  132.8 123.4 %all-gather.14.cloned.1.call-start = ((), (), s32[]{:S(2)}) async-start(), calls=%async_computation.3 | async-start | bytes 6291456 | tf_op jit(solution)/shard_map/all_gather | solution.py:61
  197.4 11.5 %copy-start.3 = (f32[8,2,64,64]{3,2,1,0:T(8,128)S(1)}, f32[8,2,64,64]{3,2,1,0:T(8,128)}, u32[]{:S(2)}) copy-start(f32[8,2,64,64]{3,2,1,0:T(8,128)} %get-tuple-element.7) | copy-start | bytes 786436
  208.8 3.0 %copy-start.1 = (f32[32,2,64,64]{3,2,1,0:T(8,128)S(1)}, f32[32,2,64,64]{3,2,1,0:T(8,128)}, u32[]{:S(2)}) copy-start(f32[32,2,64,64]{3,2,1,0:T(8,128)} %all-gather.16.cloned.1.call-done) | copy-start | bytes 3145732
  214.4 3.5 %copy-start.4 = (bf16[128,2,64,16]{0,2,1,3:T(8,128)(2,1)S(1)}, bf16[128,2,64,16]{0,2,1,3:T(8,128)(2,1)}, u32[]{:S(2)}) copy-start(bf16[128,2,64,16]{0,2,1,3:T(8,128)(2,1)} %copy.48) | copy-start | bytes 1572868
Sparse Core Ops, SparseCore 0:
  10.0 57.6 all-gather.9
  78.8 14.5 all-gather.15
  96.0 33.6 all-gather.19
  131.4 41.8 all-gather.11
  174.9 31.8 all-gather.17
  208.5 19.0 all-gather.13
where the time goes:
time: 268 us; the launch traced here: 267 us
  waiting for transfers between devices  152 us (57%)
  blocking collectives  38.7 us (14%)
  local copies, waits for them, and re-layouts  25.3 us (9%)
  matrix products  24 us (9%)
  between operations  13.8 us (5%)
  other arithmetic  13.4 us (5%)
    all_gather x1, waiting for transfers between devices, body(): piece = lax.all_gather(normed, 'cols', axis=0, tiled=True)  54.4 us
    all_gather x1, waiting for transfers between devices, body(): w_part = lax.all_gather(w_part, 'cols', axis=0, tiled=True)  40.2 us
    all_to_all x1, blocking collectives, body(): mine = lax.all_to_all(results, 'cols', 0, 2, tiled=True)  35.8 us
    all_gather x1, waiting for transfers between devices, exclusive_rows_scan(): gx = lax.all_gather(mine, 'x')  32.9 us
    all_gather x1, waiting for transfers between devices, exclusive_rows_scan(): pair = lax.all_gather(states, 'core')  14.6 us
    all_gather x1, waiting for transfers between devices, exclusive_rows_scan(): gy = lax.all_gather(xsum, 'y')  9.49 us
    squeeze x4, local copies, waits for them, and re-layouts, body(): qrow, krow, vrow = (parts[:, :, :, 0], parts[:, :, :, 1], parts[:, :, :, 2])  7.74 us
    dot_general x1, matrix products, body(): jnp.dot(piece.reshape(-1, width), w_flat, preferred_element_type=jnp.floa...  5.78 us
  transfers between devices with their start and end apart: 6, of which 5 were waited for; matrix products, arithmetic and copies ran while one was open for 16% of the time, Pallas kernels for 0%

commit v1 on v0

--- a/solution.py
+++ b/solution.py
@@ -57,7 +57,9 @@
     core = lax.axis_index("core")
     wh = width // 2
     w_part = lax.dynamic_slice_in_dim(w_out, core * wh, wh, axis=2)
-    w_part = lax.all_gather(w_part, "cols", axis=0, tiled=True)
+    w_part = jnp.concatenate(
+        lax.all_to_all(jnp.stack([w_part] * lax.axis_size("cols")), "cols", 0, 0), axis=0
+    )
     w_full = lax.all_gather(w_part, "core", axis=2, tiled=True)
     xloc = sheet.astype(jnp.float32)
     normed = (xloc * lax.rsqrt(jnp.mean(xloc * xloc, axis=-1, keepdims=True) + 1e-06)).astype(

time: 268 us -> 228 us (0.85)
  waiting for transfers between devices: 152 us -> 106 us
  starting transfers between devices: 0.39 us -> 4.67 us
    all_gather x1 -> x0, waiting for transfers between devices: 40.2 us -> none  [body(): w_part = lax.all_gather(w_part, 'cols', axis=0, tiled=True)]
    all_gather x1, waiting for transfers between devices: 14.6 us -> 8.76 us  [exclusive_rows_scan(): pair = lax.all_gather(states, 'core')]
    all_to_all x0 -> x1, starting transfers between devices: none -> 4.32 us  [body(): lax.all_to_all(jnp.stack([w_part] * lax.axis_size('cols')), 'cols', 0, 0)]
    all_gather x1, waiting for transfers between devices: 9.49 us -> 6.27 us  [exclusive_rows_scan(): gy = lax.all_gather(xsum, 'y')]
    unnamed x13 -> x15, local copies, waits for them, and re-layouts: 5.35 us -> 6.64 us
  transfers between devices with their start and end apart: 6 -> 6, of which waited for: 5 -> 5; matrix products, arithmetic and copies ran while one was open for 16% -> 20% of each run, Pallas kernels for 0% -> 0%
where the time goes in v1:
time: 228 us
  waiting for transfers between devices  106 us (46%)
  blocking collectives  38.7 us (17%)
  local copies, waits for them, and re-layouts  27.4 us (12%)
  matrix products  24.1 us (11%)
  other arithmetic  13.4 us (6%)
  between operations  13.4 us (6%)
  starting transfers between devices  4.67 us (2%)
    all_gather x1, waiting for transfers between devices, body(): piece = lax.all_gather(normed, 'cols', axis=0, tiled=True)  54.4 us
    all_to_all x1, blocking collectives, body(): mine = lax.all_to_all(results, 'cols', 0, 2, tiled=True)  35.8 us
    all_gather x1, waiting for transfers between devices, exclusive_rows_scan(): gx = lax.all_gather(mine, 'x')  33.7 us
    all_gather x1, waiting for transfers between devices, exclusive_rows_scan(): pair = lax.all_gather(states, 'core')  8.76 us
    squeeze x4, local copies, waits for them, and re-layouts, body(): qrow, krow, vrow = (parts[:, :, :, 0], parts[:, :, :, 1], parts[:, :, :, 2])  7.74 us
    unnamed x15, local copies, waits for them, and re-layouts  6.64 us
    all_gather x1, waiting for transfers between devices, exclusive_rows_scan(): gy = lax.all_gather(xsum, 'y')  6.27 us
    dot_general x1, matrix products, body(): jnp.dot(piece.reshape(-1, width), w_flat, preferred_element_type=jnp.floa...  5.78 us
  transfers between devices with their start and end apart: 6, of which 5 were waited for; matrix products, arithmetic and copies ran while one was open for 20% of the time, Pallas kernels for 0%

profile of v1, /device:TPU:2, one launch (start us, length us, event | category | flops | bytes accessed | tf_op | source)
XLA Modules:
  0.0 227.5 jit_solution(1230211027453386069)
XLA Ops:
  6.5 1.3 fusion.10
  7.8 2.0 fusion.11
  9.8 0.0 all-gather.9.cloned.1.call-update
  9.8 0.0 all-gather.13.cloned.1.call-start
  9.9 1.7 copy.59
  11.6 1.6 copy.38
  13.3 54.4 %all-gather.9.cloned.1.call-done = bf16[16,128,1024]{2,1,0:T(8,128)(2,1)} async-done(((bf16[2,128,1024]{2,1,0:T(8,128)(2,1)}), bf16[16,128,1024]{2,1,0:T(8,128)(2,1)}) %all-gather.9.cloned.1.call-update) | async-done | bytes 4194320 | tf_op jit(solution)/shard_map/all_gather | solution.py:68
  67.7 5.8 %fusion.43 = (bf16[16,128,2,6,64]{1,4,3,2,0:T(8,128)(2,1)S(1)}, f32[16,128,2,6,64]{1,4,3,2,0:T(8,128)S(1)}) fusion(bf16[2,6,64,1024,1]{3,2,1,0,4:T(8,128)(2,1)} %bitcast.64, bf16[16,128,1024]{2,1,0:T(8,128)(2,1)} %all-gather.9.cloned.1.call-done), kind=kOutput, calls=%fused_computation.67 | convolution fusion | flops 3222798336 | bytes 15204352 | tf_op jit(solution)/shard_map/dot_general | solution.py:70
  73.5 0.0 copy-start.3
  73.5 0.0 copy-start.6
  73.5 2.6 %copy-done.3 = f32[16,128,2,6,64]{1,4,3,2,0:T(8,128)} copy-done((f32[16,128,2,6,64]{1,4,3,2,0:T(8,128)}, f32[16,128,2,6,64]{1,4,3,2,0:T(8,128)S(1)}, u32[]{:S(2)}) %copy-start.3) | copy-done | bytes 6291480
  76.2 1.0 copy-done.6
  77.1 1.5 fusion.26
  78.7 0.0 all-gather.13.cloned.1.call-update
  78.7 0.0 copy-done
  78.7 1.5 stack.3
  80.2 4.3 %all-to-all-start.1 = ((bf16[8,2,128,512]{3,2,1,0:T(8,128)(2,1)}), bf16[8,2,128,512]{3,2,1,0:T(8,128)(2,1)S(1)}, u32[]{:S(2)}, u32[]{:S(2)}) async-start(bf16[8,2,128,512]{3,2,1,0:T(8,128)(2,1)} %stack.3), calls=%async_computation.1 | async-start | bytes 4194304 | tf_op jit(solution)/shard_map/all_to_all | solution.py:61
  84.6 0.0 all-gather.17.cloned.1.call-start
  84.6 8.8 %all-gather.13.cloned.1.call-done = f32[32,2,64,64]{3,2,1,0:T(8,128)} async-done(((f32[16,2,64,64]{3,2,1,0:T(8,128)}), f32[32,2,64,64]{3,2,1,0:T(8,128)}) %all-gather.13.cloned.1.call-update) | async-done | bytes 1048592 | tf_op jit(solution)/shard_map/all_gather | solution.py:38
  93.4 1.7 fusion.42
  95.0 0.9 dynamic-slice_add_fusion
  95.9 0.0 all-gather.17.cloned.1.call-update
  95.9 0.0 all-gather.15.cloned.1.call-start
  96.0 33.7 %all-gather.17.cloned.1.call-done = f32[32,2,64,64]{3,2,1,0:T(8,128)} async-done(((f32[8,2,64,64]{3,2,1,0:T(8,128)}), f32[32,2,64,64]{3,2,1,0:T(8,128)}) %all-gather.17.cloned.1.call-update) | async-done | bytes 1048592 | tf_op jit(solution)/shard_map/all_gather | solution.py:43
  129.7 3.1 %select_reduce_fusion = (f32[8,2,64,64]{3,2,1,0:T(8,128)}, f32[8,2,64,64]{3,2,1,0:T(8,128)}) fusion(f32[4,8,2,64,64]{4,3,2,1,0:T(8,128)} %bitcast.61, pred[4]{0:T(512)(128)(4,1)S(1)} %iota_compare_fusion.1), kind=kLoop, calls=%fused_computation.8 | loop fusion | flops 655360 | bytes 1572868 | tf_op jit(solution)/shard_map/reduce_sum | solution.py:32
  132.8 0.0 all-gather.15.cloned.1.call-update
  132.8 0.2 all-gather.11.cloned.1.call-start
  133.1 2.5 %all-to-all-done.1 = bf16[8,2,128,512]{3,2,1,0:T(8,128)(2,1)S(1)} async-done(((bf16[8,2,128,512]{3,2,1,0:T(8,128)(2,1)}), bf16[8,2,128,512]{3,2,1,0:T(8,128)(2,1)S(1)}, u32[]{:S(2)}, u32[]{:S(2)}) %all-to-all-start.1) | async-done | bytes 2097184 | tf_op jit(solution)/shard_map/all_to_all | solution.py:61
  135.6 1.3 copy-done.1
  136.9 0.0 all-gather.11.cloned.1.call-update
  136.9 1.9 multiply_reduce_fusion.1
  138.8 1.1 slice_bitcast_fusion.1
  140.0 1.9 fusion.21
  141.8 2.5 %copy.43 = bf16[16,128,2,64]{3,0,2,1:T(8,128)(2,1)} copy(bf16[16,128,2,64]{1,3,2,0:T(8,128)(2,1)S(1)} %get-tuple-element.10) | data formatting | bytes 1048576 | tf_op jit(solution)/shard_map/squeeze | solution.py:73
  144.4 2.5 %copy.44 = bf16[16,128,2,64]{3,0,2,1:T(8,128)(2,1)} copy(bf16[16,128,2,64]{1,3,2,0:T(8,128)(2,1)S(1)} %get-tuple-element.9) | data formatting | bytes 1048576 | tf_op jit(solution)/shard_map/squeeze | solution.py:73
  146.9 2.3 %fusion.44 = f32[128,2,16,16]{2,3,1,0:T(8,128)S(1)} fusion(bf16[16,128,2,64]{3,0,2,1:T(8,128)(2,1)} %copy.43, bf16[16,128,2,64]{3,0,2,1:T(8,128)(2,1)} %copy.44), kind=kOutput, calls=%fused_computation.68 | convolution fusion | flops 8388608 | bytes 1310720 | tf_op jit(solution)/shard_map/crhd,erhd->rhce/dot_general | solution.py:78
  149.2 1.3 copy.45
  150.6 0.1 fusion.27
  150.6 0.1 divide_convert_fusion
  150.7 1.4 copy.47
  152.2 1.6 copy.46
  153.8 1.7 fusion.45
  155.4 3.0 %copy.48 = bf16[128,2,64,16]{0,2,1,3:T(8,128)(2,1)} copy(bf16[128,2,64,16]{2,3,1,0:T(8,128)(2,1)} %fusion.45) | data formatting | bytes 1048576 | tf_op jit(solution)/shard_map/rhce,erhd->crhd/dot_general | solution.py:81
  158.4 2.6 %fusion.37 = f32[16,2,128,128]{3,2,1,0:T(8,128)S(1)} fusion(f32[16,128,2,6,64]{1,4,3,2,0:T(8,128)} %copy-done.3), kind=kOutput, calls=%fused_computation.65 | convolution fusion | flops 69730304 | bytes 4194304 | tf_op jit(solution)/shard_map/cthd,cshd->chts/dot_general | solution.py:85
  161.1 0.0 copy-start.4
  161.1 6.3 %all-gather.15.cloned.1.call-done = f32[32,2,64,64]{3,2,1,0:T(8,128)} async-done(((f32[8,2,64,64]{3,2,1,0:T(8,128)}), f32[32,2,64,64]{3,2,1,0:T(8,128)}) %all-gather.15.cloned.1.call-update) | async-done | bytes 1048592 | tf_op jit(solution)/shard_map/all_gather | solution.py:45
  167.3 2.0 select_reduce_fusion.1
  169.3 0.0 copy-start.2
  169.3 0.0 copy-done.4
  169.3 0.1 add.72
  169.4 2.9 %all_gather.31 = f32[16,2,64,64]{3,2,1,0:T(8,128)S(1)} all-gather(f32[8,2,64,64]{3,2,1,0:T(8,128)S(1)} %add.72), channel_id=1, replica_groups=mesh['y'=4,'x'=4,'core'=2,'cols'=8] {'core'}, dimensions={0}, use_global_device_ids=true | all-gather | bytes 786432 | tf_op jit(solution)/shard_map/all_gather | solution.py:47
  172.3 0.0 copy-done.2
  172.3 2.6 %fusion.18 = f32[16,2,64,128]{3,2,1,0:T(8,128)S(1)} fusion(f32[16,2,64,64]{3,2,1,0:T(8,128)S(1)} %all_gather.31, pred[]{:T(512)S(6)} %eq.3, f32[32,2,64,64]{3,2,1,0:T(8,128)S(1)} %copy-done.2, f32[16,128,2,6,64]{1,4,3,2,0:T(8,128)} %copy-done.3), kind=kOutput, calls=%fused_computation.26 | convolution fusion | flops 202899456 | bytes 4194305 | tf_op jit(solution)/shard_map/cthk,chkv->cthv/dot_general | solution.py:87
  174.9 0.0 copy-start.5
  174.9 3.3 %multiply_reduce_fusion = (f32[16,128,2]{1,2,0:T(2,128)S(1)}, f32[16,128,2,64]{1,3,2,0:T(8,128)S(1)}) fusion(f32[16,2,64,128]{3,2,1,0:T(8,128)S(1)} %fusion.18, f32[16,2,128,128]{3,2,1,0:T(8,128)S(1)} %fusion.37, f32[128,128]{1,0:T(8,128)S(1)} %fusion.28, bf16[16,128,2,6,64]{1,4,3,2,0:T(8,128)(2,1)} %copy-done.6), kind=kOutput, calls=%fused_computation.28 | convolution fusion | flops 403959808 | bytes 4800512 | tf_op jit(solution)/shard_map/chts,cshv->cthv/dot_general | solution.py:86
  178.3 0.1 multiply_convert_fusion
  178.4 0.0 copy-done.5
  178.4 0.1 pad_maximum_fusion
  178.5 0.8 copy.53
  179.3 35.8 %all_to_all.20 = bf16[16,128,2,128]{3,2,1,0:T(2,128)(2,1)S(1)} all-to-all(bf16[16,128,2,128]{3,2,1,0:T(2,128)(2,1)S(1)} %copy.53), channel_id=1, replica_groups=mesh['y'=4,'x'=4,'core'=2,'cols'=8] {'cols'}, dimensions={0} | all-to-all | bytes 2097152 | tf_op jit(solution)/shard_map/all_to_all | solution.py:90
  215.2 0.7 copy.76
  215.9 0.8 dot_general.39
  216.7 0.0 all-gather.11.cloned.1.call-done
  216.8 4.2 %convolution_convert_fusion = bf16[2,128,1024]{2,1,0:T(8,128)(2,1)} fusion(bf16[2,128,2048]{2,1,0:T(8,128)(2,1)S(1)} %dot_general.39, bf16[2048,1024,1]{1,0,2:T(8,128)(2,1)} %bitcast.65), kind=kOutput, calls=%fused_computation.14 | convolution fusion | flops 1074003968 | bytes 5767168 | tf_op jit(solution)/shard_map/dot_general | solution.py:92
  (13 shorter events, 0.1 us)
Async XLA Ops:
  6.5 72.2 %copy-start = (bf16[2,128,1024]{2,1,0:T(8,128)(2,1)S(1)}, bf16[2,128,1024]{2,1,0:T(8,128)(2,1)}, u32[]{:S(2)}) copy-start(bf16[2,128,1024]{2,1,0:T(8,128)(2,1)} %param.5) | copy-start | bytes 1572868
  6.5 61.2 %all-gather.9.cloned.1.call-start = ((), (), s32[]{:S(2)}) async-start(), calls=%async_computation.2 | async-start | bytes 4718592 | tf_op jit(solution)/shard_map/all_gather | solution.py:68
  9.8 83.5 %all-gather.13.cloned.1.call-start = ((), (), s32[]{:S(2)}) async-start(), calls=%async_computation.4 | async-start | bytes 3145728 | tf_op jit(solution)/shard_map/all_gather | solution.py:38
  73.5 2.7 %copy-start.3 = (f32[16,128,2,6,64]{1,4,3,2,0:T(8,128)}, f32[16,128,2,6,64]{1,4,3,2,0:T(8,128)S(1)}, u32[]{:S(2)}) copy-start(f32[16,128,2,6,64]{1,4,3,2,0:T(8,128)S(1)} %get-tuple-element.14) | copy-start | bytes 18874372
  73.5 3.6 %copy-start.6 = (bf16[16,128,2,6,64]{1,4,3,2,0:T(8,128)(2,1)}, bf16[16,128,2,6,64]{1,4,3,2,0:T(8,128)(2,1)S(1)}, u32[]{:S(2)}) copy-start(bf16[16,128,2,6,64]{1,4,3,2,0:T(8,128)(2,1)S(1)} %get-tuple-element.13) | copy-start | bytes 9437188
  80.2 55.4 %all-to-all-start.1 = ((bf16[8,2,128,512]{3,2,1,0:T(8,128)(2,1)}), bf16[8,2,128,512]{3,2,1,0:T(8,128)(2,1)S(1)}, u32[]{:S(2)}, u32[]{:S(2)}) async-start(bf16[8,2,128,512]{3,2,1,0:T(8,128)(2,1)} %stack.3), calls=%async_computation.1 | async-start | bytes 4194304 | tf_op jit(solution)/shard_map/all_to_all | solution.py:61
  84.6 45.2 %all-gather.17.cloned.1.call-start = ((), (), s32[]{:S(2)}) async-start(), calls=%async_computation.6 | async-start | bytes 2621440 | tf_op jit(solution)/shard_map/all_gather | solution.py:43
  95.9 71.4 %all-gather.15.cloned.1.call-start = ((), (), s32[]{:S(2)}) async-start(), calls=%async_computation.5 | async-start | bytes 2621440 | tf_op jit(solution)/shard_map/all_gather | solution.py:45
  132.8 83.9 %all-gather.11.cloned.1.call-start = ((), (), s32[]{:S(2)}) async-start(), calls=%async_computation.3 | async-start | bytes 6291456 | tf_op jit(solution)/shard_map/all_gather | solution.py:63
  135.6 1.3 copy-start.1
  161.1 8.3 %copy-start.4 = (f32[8,2,64,64]{3,2,1,0:T(8,128)S(1)}, f32[8,2,64,64]{3,2,1,0:T(8,128)}, u32[]{:S(2)}) copy-start(f32[8,2,64,64]{3,2,1,0:T(8,128)} %get-tuple-element.7) | copy-start | bytes 786436
  169.3 3.0 %copy-start.2 = (f32[32,2,64,64]{3,2,1,0:T(8,128)S(1)}, f32[32,2,64,64]{3,2,1,0:T(8,128)}, u32[]{:S(2)}) copy-start(f32[32,2,64,64]{3,2,1,0:T(8,128)} %all-gather.13.cloned.1.call-done) | copy-start | bytes 3145732
  174.9 3.5 %copy-start.5 = (bf16[128,2,64,16]{0,2,1,3:T(8,128)(2,1)S(1)}, bf16[128,2,64,16]{0,2,1,3:T(8,128)(2,1)}, u32[]{:S(2)}) copy-start(bf16[128,2,64,16]{0,2,1,3:T(8,128)(2,1)} %copy.48) | copy-start | bytes 1572868
Sparse Core Ops, SparseCore 0:
  10.0 57.6 all-gather.8
  78.8 14.5 all-gather.12
  96.0 33.6 all-gather.16
  133.0 34.3 all-gather.14
  169.0 19.0 all-gather.10
